TPU v7x, 32 devices: a whole 2x2x4 slice. The times are simulated.
32 devices in a mesh: dp: 4 (over y, x), seq: 8 (over z, core).
Axes of the slice: x: 2, y: 2, z: 4, core: 2. Of those that a mesh axis runs over, the one named last changes fastest.
Arguments:
- queries: bfloat16 [6144, 2048], P(('dp', 'seq')), may hold values from -16 to 16
- keys: bfloat16 [6144, 2048], P(('dp', 'seq')), may hold values from -16 to 16
- values: bfloat16 [6144, 2048], P(('dp', 'seq')), may hold values from -6 to 6
- out_grad: bfloat16 [6144, 2048], P(('dp', 'seq')), may hold values from -6 to 6
- out_weight: bfloat16 [2048, 2048], P('dp'), may hold values from -0.125 to 0.125
- section_ids: int32 [6144], P(('dp', 'seq')), may hold values from 0 to 95, as said below
- masked: int32 [6144], P(('dp', 'seq')), may hold values from 0 to 1, as said below
Outputs:
- query_grad: bfloat16 [6144, 2048], P(('dp', 'seq'))
- key_grad: bfloat16 [6144, 2048], P(('dp', 'seq'))
- value_grad: bfloat16 [6144, 2048], P(('dp', 'seq'))
- weight_grad: float32 [2048, 2048], P('dp')
Inputs may be any that keep to these rules, and one draw needn't show every extreme that they name: `section_ids`: section numbers never fall along the tokens, are constant over each aligned block of 64 tokens, and no section spans two sequences of 1536 tokens. `masked`: the same for all tokens of a section.
All inputs are finite; a program needn't handle non-finite values.
Results may differ from a plain program's by a relative error of at most 0.015.
Values may be sent and summed in bfloat16 or wider, within the bound.
No kernel may reach another device: no remote copies, remote signals or barrier semaphores. Data moves between devices by JAX's collectives and lax.ppermute only.
A program may use at most 128 MiB of HBM per device.

v0:
```python
import jax
import jax.numpy as jnp
from jax import lax
from jax.sharding import PartitionSpec as P

HEAD_DIM = 128


def local(queries, keys, values, out_grad, out_weight, section_ids, masked):
    score_scale = HEAD_DIM ** (-0.5)
    attn_grad = lax.dot_general(
        out_grad,
        lax.all_gather(out_weight, "dp", axis=0, tiled=True),
        (((1,), (1,)), ((), ())),
        preferred_element_type=jnp.float32,
    ).astype(jnp.bfloat16)
    query_h, key_h, value_h = (
        lax.all_to_all(queries, "seq", split_axis=1, concat_axis=0, tiled=True),
        lax.all_to_all(keys, "seq", split_axis=1, concat_axis=0, tiled=True),
        lax.all_to_all(values, "seq", split_axis=1, concat_axis=0, tiled=True),
    )
    grad_h = lax.all_to_all(attn_grad, "seq", split_axis=1, concat_axis=0, tiled=True)
    n_seq = lax.axis_size("seq")
    code = section_ids * 2 + masked
    code_all = lax.all_to_all(
        jnp.broadcast_to(code[None], (n_seq,) + code.shape), "seq", 0, 0, tiled=True
    ).reshape(-1)
    sec_all = code_all // 2
    flag_all = code_all - 2 * sec_all
    grad_plane = lax.all_gather(out_grad, "dp", axis=0, tiled=True)
    seq_span = query_h.shape[0]
    width_here = query_h.shape[1]
    heads_here = width_here // HEAD_DIM
    block_rows = min(512, seq_span)
    num_blocks = seq_span // block_rows
    keys_head = key_h.reshape(seq_span, heads_here, HEAD_DIM)
    values_head = value_h.reshape(seq_span, heads_here, HEAD_DIM)
    visible_key = flag_all == 0

    def block_step(carried, block_item):
        key_acc, value_acc = carried
        query_blk, grad_blk, sec_blk = block_item
        scores = (
            jnp.einsum("qhd,khd->hqk", query_blk, keys_head, preferred_element_type=jnp.float32)
            * score_scale
        )
        allowed = visible_key[None, :] | (sec_blk[:, None] == sec_all[None, :])
        scores = jnp.where(allowed[None], scores, -1e30)
        row_max = jnp.max(scores, axis=2, keepdims=True)
        exp_scores = jnp.exp(scores - row_max)
        attn_probs = exp_scores / jnp.sum(exp_scores, axis=2, keepdims=True)
        probs_low = attn_probs.astype(jnp.bfloat16)
        out_blk = jnp.einsum(
            "hqk,khd->qhd", probs_low, values_head, preferred_element_type=jnp.float32
        ).astype(jnp.bfloat16)
        row_delta = jnp.sum(grad_blk.astype(jnp.float32) * out_blk.astype(jnp.float32), axis=2)
        prob_grad = jnp.einsum(
            "qhd,khd->hqk", grad_blk, values_head, preferred_element_type=jnp.float32
        )
        score_grad = (attn_probs * (prob_grad - row_delta.T[:, :, None])).astype(jnp.bfloat16)
        query_blk_grad = (
            jnp.einsum("hqk,khd->qhd", score_grad, keys_head, preferred_element_type=jnp.float32)
            * score_scale
        ).astype(jnp.bfloat16)
        key_acc = key_acc + jnp.einsum(
            "hqk,qhd->khd", score_grad, query_blk, preferred_element_type=jnp.float32
        )
        value_acc = value_acc + jnp.einsum(
            "hqk,qhd->khd", probs_low, grad_blk, preferred_element_type=jnp.float32
        )
        return ((key_acc, value_acc), (out_blk, query_blk_grad))

    scan_inputs = (
        query_h.reshape(num_blocks, block_rows, heads_here, HEAD_DIM),
        grad_h.reshape(num_blocks, block_rows, heads_here, HEAD_DIM),
        sec_all.reshape(num_blocks, block_rows),
    )
    zero_acc = jnp.zeros((seq_span, heads_here, HEAD_DIM), jnp.float32)
    (key_acc, value_acc), (out_blocks, query_blocks) = lax.scan(
        block_step, (zero_acc, zero_acc), scan_inputs
    )
    out_head = out_blocks.reshape(seq_span, width_here)
    query_grad_h = query_blocks.reshape(seq_span, width_here)
    key_grad_h = (key_acc * score_scale).astype(jnp.bfloat16).reshape(seq_span, width_here)
    value_grad_h = value_acc.astype(jnp.bfloat16).reshape(seq_span, width_here)
    attn_out, query_grad, key_grad, value_grad = (
        lax.all_to_all(out_head, "seq", split_axis=0, concat_axis=1, tiled=True),
        lax.all_to_all(query_grad_h, "seq", split_axis=0, concat_axis=1, tiled=True),
        lax.all_to_all(key_grad_h, "seq", split_axis=0, concat_axis=1, tiled=True),
        lax.all_to_all(value_grad_h, "seq", split_axis=0, concat_axis=1, tiled=True),
    )
    out_plane = lax.all_to_all(attn_out, "dp", split_axis=1, concat_axis=0, tiled=True)
    weight_grad = lax.psum(
        lax.dot_general(
            out_plane, grad_plane, (((0,), (0,)), ((), ())), preferred_element_type=jnp.float32
        ),
        "seq",
    )
    return (query_grad, key_grad, value_grad, weight_grad)


def solution(mesh):
    placed = (
        P(("dp", "seq"), None),
        P(("dp", "seq"), None),
        P(("dp", "seq"), None),
        P(("dp", "seq"), None),
        P("dp", None),
        P(("dp", "seq")),
        P(("dp", "seq")),
    )
    return jax.shard_map(
        local,
        mesh=mesh,
        in_specs=placed,
        out_specs=(
            P(("dp", "seq"), None),
            P(("dp", "seq"), None),
            P(("dp", "seq"), None),
            P("dp", None),
        ),
        check_vma=False,
    )
```

profile of v0, /device:TPU:0, one launch (start us, length us, event | category | flops | bytes accessed | tf_op | source)
XLA Modules:
  0.0 405.7 jit_solution(10119106563263983084)
XLA Ops:
  9.2 6.4 %all-to-all-start.1 = ((s32[8,1,192]{2,1,0:T(1,128)}), s32[8,1,192]{2,1,0:T(1,128)S(1)}, u32[]{:S(2)}, u32[]{:S(2)}) async-start(s32[8,1,192]{2,1,0:T(1,128)} %broadcast_in_dim.36), calls=%async_computation.1 | async-start | bytes 16384 | tf_op jit(solution)/shard_map/all_to_all | solution.py:25
  15.6 2.1 copy.117
  17.7 3.5 all-to-all-done.1
  21.2 3.6 all-to-all-start.2
  25.7 19.9 %all-to-all-done.2 = bf16[192,8,256]{2,0,1:T(8,128)(2,1)S(1)} async-done(((bf16[192,8,256]{2,0,1:T(8,128)(2,1)}), bf16[192,8,256]{2,0,1:T(8,128)(2,1)S(1)}, u32[]{:S(2)}, u32[]{:S(2)}) %all-to-all-start.2) | async-done | bytes 786464 | tf_op jit(solution)/shard_map/all_to_all | solution.py:19
  45.6 3.5 all-to-all-start.4
  49.2 0.9 copy.118
  50.1 19.9 %all-to-all-done.4 = bf16[192,8,256]{2,0,1:T(8,128)(2,1)S(1)} async-done(((bf16[192,8,256]{2,0,1:T(8,128)(2,1)}), bf16[192,8,256]{2,0,1:T(8,128)(2,1)S(1)}, u32[]{:S(2)}, u32[]{:S(2)}) %all-to-all-start.4) | async-done | bytes 786464 | tf_op jit(solution)/shard_map/all_to_all | solution.py:20
  70.1 3.5 all-to-all-start
  73.6 26.4 %all-gather.3.cloned.1.call-done = bf16[2048,2048]{1,0:T(8,128)(2,1)} async-done(((bf16[512,2048]{1,0:T(8,128)(2,1)}), bf16[2048,2048]{1,0:T(8,128)(2,1)}) %all-gather.3.cloned.1.call-update) | async-done | bytes 8388624 | tf_op jit(solution)/shard_map/all_gather | solution.py:13
  100.1 6.5 %convolution_convert_fusion.1 = bf16[192,2048]{1,0:T(8,128)(2,1)S(1)} fusion(bf16[192,2048]{1,0:T(8,128)(2,1)} %param.12, bf16[2048,2048]{1,0:T(8,128)(2,1)} %all-gather.3.cloned.1.call-done), kind=kOutput, calls=%fused_computation.31 | convolution fusion | flops 1611005952 | bytes 9961472 | tf_op jit(solution)/shard_map/dot_general | solution.py:11
  106.6 0.9 copy.116
  107.6 4.6 %all-to-all-start.3 = ((bf16[192,8,256]{2,0,1:T(8,128)(2,1)}), bf16[192,8,256]{2,0,1:T(8,128)(2,1)}, u32[]{:S(2)}, u32[]{:S(2)}) async-start(bf16[192,8,256]{2,0,1:T(8,128)(2,1)} %bitcast.76), calls=%async_computation.3 | async-start | bytes 1572864 | tf_op jit(solution)/shard_map/all_to_all | solution.py:22
  113.7 1.8 copy.68
  115.7 17.5 %all-to-all-done.3 = bf16[192,8,256]{2,0,1:T(8,128)(2,1)} async-done(((bf16[192,8,256]{2,0,1:T(8,128)(2,1)}), bf16[192,8,256]{2,0,1:T(8,128)(2,1)}, u32[]{:S(2)}, u32[]{:S(2)}) %all-to-all-start.3) | async-done | bytes 786464 | tf_op jit(solution)/shard_map/all_to_all | solution.py:22
  133.2 2.0 reshape.128
  135.2 65.2 %while.17 = (s32[]{:T(128)}, f32[1536,2,128]{0,2,1:T(8,128)}, f32[1536,2,128]{0,2,1:T(8,128)}, bf16[3,512,2,128]{3,2,1,0:T(2,128)(2,1)}, bf16[3,512,2,128]{3,2,1...) while((s32[]{:T(128)}, f32[1536,2,128]{0,2,1:T(8,128)}, ...), condition=%wide.region_4.5_spmd.clone, body=%wide.region_0.4_spmd.clone.sunk | while | flops 2435711488 | bytes 120883744 | solution.py:79
  136.1 5.0 %fusion.54 = (f32[2,512]{1,0:T(2,128)S(1)}, f32[2,512,1536]{2,1,0:T(8,128)}) fusion(pred[512,1536]{1,0:T(8,128)(4,1)S(1)} %compare_or_fusion.2, bf16[1536,2,128]{2,0,1:T(8,128)(2,1)S(1)} %get-tuple-element.300, bf16[1,512,2,128]{3,2,1,0:T(2,128)(2,1)S(1)} %constant_dynamic-slice_fusion.8), kind=kOutput, calls=%fused_computation.53.clone.1 | convolution fusion | flops 408946176 | bytes 8130560 | tf_op jit(solution)/shard_map/while/body/eval_jaxpr/sub | solution.py:50
  141.1 3.8 fusion.55
  145.1 1.1 multiply_reduce_fusion.2
  146.2 1.2 multiply_convert_fusion.3
  147.5 2.1 fusion.58
  149.6 1.3 copy_dynamic-update-slice_fusion.3
  150.9 1.8 fusion.56
  153.4 1.9 fusion.57
  156.2 5.0 %fusion.54 = (f32[2,512]{1,0:T(2,128)S(1)}, f32[2,512,1536]{2,1,0:T(8,128)}) fusion(pred[512,1536]{1,0:T(8,128)(4,1)S(1)} %compare_or_fusion.2, bf16[1536,2,128]{2,0,1:T(8,128)(2,1)S(1)} %get-tuple-element.300, bf16[1,512,2,128]{3,2,1,0:T(2,128)(2,1)S(1)} %constant_dynamic-slice_fusion.8), kind=kOutput, calls=%fused_computation.53.clone.1 | convolution fusion | flops 408946176 | bytes 8130560 | tf_op jit(solution)/shard_map/while/body/eval_jaxpr/sub | solution.py:50
  161.2 3.8 fusion.55
  165.2 1.1 multiply_reduce_fusion.2
  166.3 1.2 multiply_convert_fusion.3
  167.6 2.1 fusion.58
  169.7 1.3 copy_dynamic-update-slice_fusion.3
  171.0 3.3 fusion.56
  174.4 3.5 fusion.57
  178.7 5.0 %fusion.54 = (f32[2,512]{1,0:T(2,128)S(1)}, f32[2,512,1536]{2,1,0:T(8,128)}) fusion(pred[512,1536]{1,0:T(8,128)(4,1)S(1)} %compare_or_fusion.2, bf16[1536,2,128]{2,0,1:T(8,128)(2,1)S(1)} %get-tuple-element.300, bf16[1,512,2,128]{3,2,1,0:T(2,128)(2,1)S(1)} %constant_dynamic-slice_fusion.8), kind=kOutput, calls=%fused_computation.53.clone.1 | convolution fusion | flops 408946176 | bytes 8130560 | tf_op jit(solution)/shard_map/while/body/eval_jaxpr/sub | solution.py:50
  183.7 3.8 fusion.55
  187.8 1.1 multiply_reduce_fusion.2
  188.9 1.2 multiply_convert_fusion.3
  190.1 2.1 fusion.58
  192.3 1.3 copy_dynamic-update-slice_fusion.3
  193.6 3.3 fusion.56
  196.9 3.5 fusion.57
  200.4 3.3 all_to_all.145
  203.7 3.8 all-to-all-start.8
  208.2 1.4 all_to_all.137
  209.6 18.5 %all-to-all-done.8 = bf16[8,192,256]{2,1,0:T(8,128)(2,1)S(1)} async-done(((bf16[8,192,256]{2,1,0:T(8,128)(2,1)}), bf16[8,192,256]{2,1,0:T(8,128)(2,1)S(1)}, u32[]{:S(2)}, u32[]{:S(2)}) %all-to-all-start.8) | async-done | bytes 786464 | tf_op jit(solution)/shard_map/all_to_all | solution.py:87
  228.1 3.5 all-to-all-start.6
  232.6 1.0 copy.77
  233.6 18.9 %all-to-all-done.6 = bf16[8,192,256]{2,1,0:T(8,128)(2,1)S(1)} async-done(((bf16[8,192,256]{2,1,0:T(8,128)(2,1)}), bf16[8,192,256]{2,1,0:T(8,128)(2,1)S(1)}, u32[]{:S(2)}, u32[]{:S(2)}) %all-to-all-start.6) | async-done | bytes 786464 | tf_op jit(solution)/shard_map/all_to_all | solution.py:89
  252.5 3.5 all-to-all-start.9
  256.0 1.5 convert_element_type.35
  258.1 1.4 all_to_all.141
  259.5 7.3 %all-to-all-done.9 = bf16[192,4,512]{2,0,1:T(8,128)(2,1)S(1)} async-done(((bf16[192,4,512]{2,0,1:T(8,128)(2,1)}), bf16[192,4,512]{2,0,1:T(8,128)(2,1)S(1)}, u32[]{:S(2)}, u32[]{:S(2)}) %all-to-all-start.9) | async-done | bytes 786464 | tf_op jit(solution)/shard_map/all_to_all | solution.py:92
  266.8 3.5 all-to-all-start.7
  270.5 5.7 %fusion.20 = f32[512,2048]{1,0:T(8,128)} fusion(bf16[768,512]{1,0:T(8,128)(2,1)S(1)} %bitcast.122, bf16[768,2048]{1,0:T(8,128)(2,1)} %all-gather.5.cloned.1.call-done), kind=kOutput, calls=%fused_computation.54 | convolution fusion | flops 1610612736 | bytes 8126464 | tf_op jit(solution)/shard_map/dot_general | solution.py:94
  276.2 1.1 copy-done.14
  277.3 1.4 all_to_all.133
  278.7 16.3 %all-to-all-done.7 = bf16[8,192,256]{2,1,0:T(8,128)(2,1)S(1)} async-done(((bf16[8,192,256]{2,1,0:T(8,128)(2,1)}), bf16[8,192,256]{2,1,0:T(8,128)(2,1)S(1)}, u32[]{:S(2)}, u32[]{:S(2)}) %all-to-all-start.7) | async-done | bytes 786464 | tf_op jit(solution)/shard_map/all_to_all | solution.py:90
  295.0 3.5 all-to-all-start.5
  298.5 1.0 copy.93
  299.5 1.0 copy.94
  300.5 27.8 %all-to-all-done.5 = bf16[8,192,256]{2,1,0:T(8,128)(2,1)S(1)} async-done(((bf16[8,192,256]{2,1,0:T(8,128)(2,1)}), bf16[8,192,256]{2,1,0:T(8,128)(2,1)S(1)}, u32[]{:S(2)}, u32[]{:S(2)}) %all-to-all-start.5) | async-done | bytes 786464 | tf_op jit(solution)/shard_map/all_to_all | solution.py:88
  328.2 1.0 copy.92
  329.2 65.3 %all-reduce.2.cloned.1.call-done = f32[512,2048]{1,0:T(8,128)} async-done(((f32[512,2048]{1,0:T(8,128)}), f32[512,2048]{1,0:T(8,128)}) %all-reduce.2.cloned.1.call-update) | async-done | bytes 4194320 | tf_op jit(solution)/shard_map/psum | solution.py:93
  394.5 4.7 %copy.149 = f32[512,2048]{1,0:T(8,128)} copy(f32[512,2048]{1,0:T(8,128)} %all-reduce.2.cloned.1.call-done) | data formatting | bytes 8388608
  (130 shorter events, 10.7 us)
Async XLA Ops:
  7.2 17.6 %copy-start.11 = (bf16[192,2048]{1,0:T(8,128)(2,1)S(1)}, bf16[192,2048]{1,0:T(8,128)(2,1)}, u32[]{:S(2)}) copy-start(bf16[192,2048]{1,0:T(8,128)(2,1)} %param.11) | copy-start | bytes 2359300
  7.2 92.9 %all-gather.3.cloned.1.call-start = ((), (), s32[]{:S(2)}) async-start(), calls=%async_computation.10 | async-start | bytes 10485760 | tf_op jit(solution)/shard_map/all_gather | solution.py:13
  9.2 12.0 %all-to-all-start.1 = ((s32[8,1,192]{2,1,0:T(1,128)}), s32[8,1,192]{2,1,0:T(1,128)S(1)}, u32[]{:S(2)}, u32[]{:S(2)}) async-start(s32[8,1,192]{2,1,0:T(1,128)} %broadcast_in_dim.36), calls=%async_computation.1 | async-start | bytes 16384 | tf_op jit(solution)/shard_map/all_to_all | solution.py:25
  15.6 33.6 %copy-start.12 = (bf16[192,2048]{1,0:T(8,128)(2,1)S(1)}, bf16[192,2048]{1,0:T(8,128)(2,1)}, u32[]{:S(2)}) copy-start(bf16[192,2048]{1,0:T(8,128)(2,1)} %param.9) | copy-start | bytes 2359300
  21.2 24.5 %all-to-all-start.2 = ((bf16[192,8,256]{2,0,1:T(8,128)(2,1)}), bf16[192,8,256]{2,0,1:T(8,128)(2,1)S(1)}, u32[]{:S(2)}, u32[]{:S(2)}) async-start(bf16[192,8,256]{2,0,1:T(8,128)(2,1)} %bitcast.77), calls=%async_computation.2 | async-start | bytes 1572864 | tf_op jit(solution)/shard_map/all_to_all | solution.py:19
  45.6 24.4 %all-to-all-start.4 = ((bf16[192,8,256]{2,0,1:T(8,128)(2,1)}), bf16[192,8,256]{2,0,1:T(8,128)(2,1)S(1)}, u32[]{:S(2)}, u32[]{:S(2)}) async-start(bf16[192,8,256]{2,0,1:T(8,128)(2,1)} %bitcast.75), calls=%async_computation.4 | async-start | bytes 1572864 | tf_op jit(solution)/shard_map/all_to_all | solution.py:20
  70.1 37.5 %all-to-all-start = ((bf16[192,8,256]{2,0,1:T(8,128)(2,1)}), bf16[192,8,256]{2,0,1:T(8,128)(2,1)S(1)}, u32[]{:S(2)}, u32[]{:S(2)}) async-start(bf16[192,8,256]{2,0,1:T(8,128)(2,1)} %bitcast.78), calls=%async_computation | async-start | bytes 1572864 | tf_op jit(solution)/shard_map/all_to_all | solution.py:18
  107.6 25.7 %all-to-all-start.3 = ((bf16[192,8,256]{2,0,1:T(8,128)(2,1)}), bf16[192,8,256]{2,0,1:T(8,128)(2,1)}, u32[]{:S(2)}, u32[]{:S(2)}) async-start(bf16[192,8,256]{2,0,1:T(8,128)(2,1)} %bitcast.76), calls=%async_computation.3 | async-start | bytes 1572864 | tf_op jit(solution)/shard_map/all_to_all | solution.py:22
  112.2 158.3 %all-gather.5.cloned.1.call-start = ((), (), s32[]{:S(2)}) async-start(), calls=%async_computation.11 | async-start | bytes 3932160 | tf_op jit(solution)/shard_map/all_gather | solution.py:30
  135.2 5.8 %copy-start.3 = (bf16[1536,2,128]{2,0,1:T(8,128)(2,1)}, bf16[1536,2,128]{2,0,1:T(8,128)(2,1)S(1)}, u32[]{:S(2)}) copy-start(bf16[1536,2,128]{2,0,1:T(8,128)(2,1)S(1)} %get-tuple-element.300) | copy-start | bytes 2359300 | tf_op jit(solution)/shard_map/while
  135.3 5.8 %copy-start.7 = (bf16[3,512,2,128]{3,2,1,0:T(2,128)(2,1)}, bf16[3,512,2,128]{3,2,1,0:T(2,128)(2,1)S(1)}, u32[]{:S(2)}) copy-start(bf16[3,512,2,128]{3,2,1,0:T(2,128)(2,1)S(1)} %get-tuple-element.296) | copy-start | bytes 2359300 | tf_op jit(solution)/shard_map/while
  135.3 9.6 %copy-start.9 = (bf16[3,512,2,128]{3,2,1,0:T(2,128)(2,1)}, bf16[3,512,2,128]{3,2,1,0:T(2,128)(2,1)S(1)}, u32[]{:S(2)}) copy-start(bf16[3,512,2,128]{3,2,1,0:T(2,128)(2,1)S(1)} %get-tuple-element.301) | copy-start | bytes 2359300 | tf_op jit(solution)/shard_map/while
  141.1 5.1 %slice-start = ((s8[6291456]{0:T(1024)(128)(4,1)}), s8[4194304]{0:T(1024)(128)(4,1)S(1)}, s32[]{:S(2)}) async-start(s8[6291456]{0:T(1024)(128)(4,1)} %bitcast.119), calls=%async_computation.13 | async-start | bytes 8388608 | tf_op jit(solution)/shard_map/while
  141.1 4.0 copy-start.13
  141.1 5.1 %slice-start.1 = ((s8[6291456]{0:T(1024)(128)(4,1)}), s8[2097152]{0:T(1024)(128)(4,1)S(1)}, s32[]{:S(2)}) async-start(s8[6291456]{0:T(1024)(128)(4,1)} %bitcast.119), calls=%async_computation.14 | async-start | bytes 4194304 | tf_op jit(solution)/shard_map/while
  144.9 2.6 copy-start
  145.1 2.4 copy-start.5
  150.9 2.5 copy-start.1
  150.9 2.5 copy-start.6
  153.4 1.9 copy-start.4
  153.4 1.9 copy-start.8
  153.4 1.9 copy-start.10
  155.3 5.8 %copy-start.3 = (bf16[1536,2,128]{2,0,1:T(8,128)(2,1)}, bf16[1536,2,128]{2,0,1:T(8,128)(2,1)S(1)}, u32[]{:S(2)}) copy-start(bf16[1536,2,128]{2,0,1:T(8,128)(2,1)S(1)} %get-tuple-element.300) | copy-start | bytes 2359300 | tf_op jit(solution)/shard_map/while
  155.3 5.8 %copy-start.7 = (bf16[3,512,2,128]{3,2,1,0:T(2,128)(2,1)}, bf16[3,512,2,128]{3,2,1,0:T(2,128)(2,1)S(1)}, u32[]{:S(2)}) copy-start(bf16[3,512,2,128]{3,2,1,0:T(2,128)(2,1)S(1)} %get-tuple-element.296) | copy-start | bytes 2359300 | tf_op jit(solution)/shard_map/while
  155.3 9.6 %copy-start.9 = (bf16[3,512,2,128]{3,2,1,0:T(2,128)(2,1)}, bf16[3,512,2,128]{3,2,1,0:T(2,128)(2,1)S(1)}, u32[]{:S(2)}) copy-start(bf16[3,512,2,128]{3,2,1,0:T(2,128)(2,1)S(1)} %get-tuple-element.301) | copy-start | bytes 2359300 | tf_op jit(solution)/shard_map/while
  161.2 5.1 %slice-start = ((s8[6291456]{0:T(1024)(128)(4,1)}), s8[4194304]{0:T(1024)(128)(4,1)S(1)}, s32[]{:S(2)}) async-start(s8[6291456]{0:T(1024)(128)(4,1)} %bitcast.119), calls=%async_computation.13 | async-start | bytes 8388608 | tf_op jit(solution)/shard_map/while
  161.2 4.0 copy-start.13
  161.2 5.1 %slice-start.1 = ((s8[6291456]{0:T(1024)(128)(4,1)}), s8[2097152]{0:T(1024)(128)(4,1)S(1)}, s32[]{:S(2)}) async-start(s8[6291456]{0:T(1024)(128)(4,1)} %bitcast.119), calls=%async_computation.14 | async-start | bytes 4194304 | tf_op jit(solution)/shard_map/while
  165.0 2.6 copy-start
  165.2 2.4 copy-start.5
  171.0 3.4 copy-start.1
  171.0 3.4 copy-start.6
  174.4 3.5 copy-start.4
  174.4 3.5 copy-start.8
  174.4 3.5 copy-start.10
  177.9 5.8 %copy-start.3 = (bf16[1536,2,128]{2,0,1:T(8,128)(2,1)}, bf16[1536,2,128]{2,0,1:T(8,128)(2,1)S(1)}, u32[]{:S(2)}) copy-start(bf16[1536,2,128]{2,0,1:T(8,128)(2,1)S(1)} %get-tuple-element.300) | copy-start | bytes 2359300 | tf_op jit(solution)/shard_map/while
  177.9 5.8 %copy-start.7 = (bf16[3,512,2,128]{3,2,1,0:T(2,128)(2,1)}, bf16[3,512,2,128]{3,2,1,0:T(2,128)(2,1)S(1)}, u32[]{:S(2)}) copy-start(bf16[3,512,2,128]{3,2,1,0:T(2,128)(2,1)S(1)} %get-tuple-element.296) | copy-start | bytes 2359300 | tf_op jit(solution)/shard_map/while
  177.9 9.6 %copy-start.9 = (bf16[3,512,2,128]{3,2,1,0:T(2,128)(2,1)}, bf16[3,512,2,128]{3,2,1,0:T(2,128)(2,1)S(1)}, u32[]{:S(2)}) copy-start(bf16[3,512,2,128]{3,2,1,0:T(2,128)(2,1)S(1)} %get-tuple-element.301) | copy-start | bytes 2359300 | tf_op jit(solution)/shard_map/while
  183.7 5.1 %slice-start = ((s8[6291456]{0:T(1024)(128)(4,1)}), s8[4194304]{0:T(1024)(128)(4,1)S(1)}, s32[]{:S(2)}) async-start(s8[6291456]{0:T(1024)(128)(4,1)} %bitcast.119), calls=%async_computation.13 | async-start | bytes 8388608 | tf_op jit(solution)/shard_map/while
  183.7 4.0 copy-start.13
  183.7 5.1 %slice-start.1 = ((s8[6291456]{0:T(1024)(128)(4,1)}), s8[2097152]{0:T(1024)(128)(4,1)S(1)}, s32[]{:S(2)}) async-start(s8[6291456]{0:T(1024)(128)(4,1)} %bitcast.119), calls=%async_computation.14 | async-start | bytes 4194304 | tf_op jit(solution)/shard_map/while
  187.5 2.6 copy-start
  187.7 2.4 copy-start.5
  193.6 3.3 copy-start.1
  193.6 3.3 copy-start.6
  196.9 3.5 copy-start.4
  196.9 3.5 copy-start.8
  196.9 3.5 copy-start.10
  200.4 7.0 %copy-start.2 = (f32[1536,2,128]{0,2,1:T(8,128)S(1)}, f32[1536,2,128]{0,2,1:T(8,128)}, u32[]{:S(2)}) copy-start(f32[1536,2,128]{0,2,1:T(8,128)} %get-tuple-element.70) | copy-start | bytes 4718596
  203.7 24.4 %all-to-all-start.8 = ((bf16[8,192,256]{2,1,0:T(8,128)(2,1)}), bf16[8,192,256]{2,1,0:T(8,128)(2,1)S(1)}, u32[]{:S(2)}, u32[]{:S(2)}) async-start(bf16[8,192,256]{2,1,0:T(8,128)(2,1)} %all_to_all.145), calls=%async_computation.8 | async-start | bytes 1572864 | tf_op jit(solution)/shard_map/all_to_all | solution.py:87
  228.1 24.4 %all-to-all-start.6 = ((bf16[8,192,256]{2,1,0:T(8,128)(2,1)}), bf16[8,192,256]{2,1,0:T(8,128)(2,1)S(1)}, u32[]{:S(2)}, u32[]{:S(2)}) async-start(bf16[8,192,256]{2,1,0:T(8,128)(2,1)} %all_to_all.137), calls=%async_computation.6 | async-start | bytes 1572864 | tf_op jit(solution)/shard_map/all_to_all | solution.py:89
  252.5 14.3 %all-to-all-start.9 = ((bf16[192,4,512]{2,0,1:T(8,128)(2,1)}), bf16[192,4,512]{2,0,1:T(8,128)(2,1)S(1)}, u32[]{:S(2)}, u32[]{:S(2)}) async-start(bf16[192,4,512]{2,0,1:T(8,128)(2,1)} %copy.77), calls=%async_computation.9 | async-start | bytes 1572864 | tf_op jit(solution)/shard_map/all_to_all | solution.py:92
  266.8 28.1 %all-to-all-start.7 = ((bf16[8,192,256]{2,1,0:T(8,128)(2,1)}), bf16[8,192,256]{2,1,0:T(8,128)(2,1)S(1)}, u32[]{:S(2)}, u32[]{:S(2)}) async-start(bf16[8,192,256]{2,1,0:T(8,128)(2,1)} %all_to_all.141), calls=%async_computation.7 | async-start | bytes 1572864 | tf_op jit(solution)/shard_map/all_to_all | solution.py:90
  270.4 124.1 %all-reduce.2.cloned.1.call-start = ((), (), s32[]{:S(2)}) async-start(), calls=%async_computation.12 | async-start | bytes 8388608 | tf_op jit(solution)/shard_map/psum | solution.py:93
  276.2 1.1 copy-start.14
  295.0 33.3 %all-to-all-start.5 = ((bf16[8,192,256]{2,1,0:T(8,128)(2,1)}), bf16[8,192,256]{2,1,0:T(8,128)(2,1)S(1)}, u32[]{:S(2)}, u32[]{:S(2)}) async-start(bf16[8,192,256]{2,1,0:T(8,128)(2,1)} %all_to_all.133), calls=%async_computation.5 | async-start | bytes 1572864 | tf_op jit(solution)/shard_map/all_to_all | solution.py:88
Sparse Core Ops, SparseCore 0:
  9.8 90.1 all-gather.2
  114.8 44.3 all-gather.4
  276.3 118.0 all-reduce.1
where the time goes:
time: 407 us; the launch traced here: 406 us
  waiting for transfers between devices  243 us (60%)
  matrix products  57.8 us (14%)
  starting transfers between devices  39.8 us (10%)
  local copies, waits for them, and re-layouts  35.5 us (9%)
  other arithmetic  15.4 us (4%)
  between operations  14 us (3%)
    psum x1, waiting for transfers between devices, local(): lax.psum(lax.dot_general(out_plane, grad_plane, (((0,), (0,)), ((), ())),...  65.3 us
    all_to_all x1, waiting for transfers between devices, local(): lax.all_to_all(query_grad_h, 'seq', split_axis=0, concat_axis=1, tiled=True)  27.8 us
    all_gather x1, waiting for transfers between devices, local(): lax.all_gather(out_weight, 'dp', axis=0, tiled=True)  26.4 us
    all_to_all x1, waiting for transfers between devices, local(): lax.all_to_all(keys, 'seq', split_axis=1, concat_axis=0, tiled=True)  19.9 us
    all_to_all x1, waiting for transfers between devices, local(): lax.all_to_all(values, 'seq', split_axis=1, concat_axis=0, tiled=True)  19.9 us
    all_to_all x1, waiting for transfers between devices, local(): lax.all_to_all(key_grad_h, 'seq', split_axis=0, concat_axis=1, tiled=True)  18.9 us
    all_to_all x1, waiting for transfers between devices, local(): lax.all_to_all(out_head, 'seq', split_axis=0, concat_axis=1, tiled=True)  18.5 us
    all_to_all x1, waiting for transfers between devices, local(): lax.all_to_all(attn_grad, 'seq', split_axis=1, concat_axis=0, tiled=True)  17.5 us
  transfers between devices with their start and end apart: 13, of which 11 were waited for; matrix products, arithmetic and copies ran while one was open for 23% of the time, Pallas kernels for 0%

commit v1 on v0

--- a/solution.py
+++ b/solution.py
@@ -4,6 +4,28 @@
 from jax.sharding import PartitionSpec as P
 
 HEAD_DIM = 128
+
+
+def split_up(x, dim, size):
+    before, after = (x.shape[:dim], x.shape[dim + 1 :])
+    return jnp.moveaxis(x.reshape(*before, size, -1, *after), dim, 0)
+
+
+def joined_along(parts, dim):
+    shape = list(parts.shape[1:])
+    shape[dim] *= parts.shape[0]
+    return jnp.moveaxis(parts, 0, dim).reshape(shape)
+
+
+def swapped_with_each(x, axis, split_dim, concat_dim):
+    peers, index = (lax.axis_size(axis), lax.axis_index(axis))
+    blocks = split_up(x, split_dim, peers)
+    outs = [blocks[index]]
+    for step in range(1, peers):
+        sent = blocks[index ^ step]
+        outs.append(lax.ppermute(sent, axis, [(i, i ^ step) for i in range(peers)]))
+    blocks = jnp.stack(outs)[index ^ jnp.arange(peers)]
+    return joined_along(blocks, concat_dim)
 
 
 def local(queries, keys, values, out_grad, out_weight, section_ids, masked):
@@ -84,7 +106,7 @@
     key_grad_h = (key_acc * score_scale).astype(jnp.bfloat16).reshape(seq_span, width_here)
     value_grad_h = value_acc.astype(jnp.bfloat16).reshape(seq_span, width_here)
     attn_out, query_grad, key_grad, value_grad = (
-        lax.all_to_all(out_head, "seq", split_axis=0, concat_axis=1, tiled=True),
+        swapped_with_each(out_head, "seq", 0, 1),
         lax.all_to_all(query_grad_h, "seq", split_axis=0, concat_axis=1, tiled=True),
         lax.all_to_all(key_grad_h, "seq", split_axis=0, concat_axis=1, tiled=True),
         lax.all_to_all(value_grad_h, "seq", split_axis=0, concat_axis=1, tiled=True),

time: 407 us -> 421 us (1.034)
  waiting for transfers between devices: 243 us -> 230 us
  matrix products: 57.8 us -> 68.8 us
  local copies, waits for them, and re-layouts: 35.5 us -> 44.4 us
  starting transfers between devices: 39.8 us -> 46.9 us
    all_to_all x1, waiting for transfers between devices: 19.9 us -> 0.01 us  [local(): lax.all_to_all(values, 'seq', split_axis=1, concat_axis=0, tiled=True)]
    all_to_all x1, waiting for transfers between devices: 0.01 us -> 19.9 us  [local(): lax.all_to_all(queries, 'seq', split_axis=1, concat_axis=0, tiled=True)]
    all_to_all x1 -> x0, waiting for transfers between devices: 18.5 us -> none  [local(): lax.all_to_all(out_head, 'seq', split_axis=0, concat_axis=1, tiled=True)]
    all_to_all x1, waiting for transfers between devices: 27.8 us -> 16.3 us  [local(): lax.all_to_all(query_grad_h, 'seq', split_axis=0, concat_axis=1, tiled=True)]
    all_to_all x1, waiting for transfers between devices: 16.3 us -> 26.6 us  [local(): lax.all_to_all(value_grad_h, 'seq', split_axis=0, concat_axis=1, tiled=True)]
    ppermute x0 -> x7, waiting for transfers between devices: none -> 9.59 us  [swapped_with_each(): outs.append(lax.ppermute(sent, axis, [(i, i ^ step) for i in range(peers)]))]
    ppermute x0 -> x7, starting transfers between devices: none -> 8.16 us  [swapped_with_each(): outs.append(lax.ppermute(sent, axis, [(i, i ^ step) for i in range(peers)]))]
    dot_general x3, matrix products: 3.27 us -> 10.3 us  [block_step(): jnp.einsum('hqk,khd->qhd', probs_low, values_head, preferred_element_type...]
  transfers between devices with their start and end apart: 13 -> 19, of which waited for: 11 -> 12; matrix products, arithmetic and copies ran while one was open for 23% -> 28% of each run, Pallas kernels for 0% -> 0%
where the time goes in v1:
time: 421 us; the launch traced here: 420 us
  waiting for transfers between devices  230 us (55%)
  matrix products  68.8 us (16%)
  starting transfers between devices  46.9 us (11%)
  local copies, waits for them, and re-layouts  44.4 us (11%)
  other arithmetic  14.9 us (4%)
  between operations  14.1 us (3%)
    psum x1, waiting for transfers between devices, local(): lax.psum(lax.dot_general(out_plane, grad_plane, (((0,), (0,)), ((), ())),...  65.1 us
    all_to_all x1, waiting for transfers between devices, local(): lax.all_to_all(value_grad_h, 'seq', split_axis=0, concat_axis=1, tiled=True)  26.6 us
    all_gather x1, waiting for transfers between devices, local(): lax.all_gather(out_weight, 'dp', axis=0, tiled=True)  26.4 us
    all_to_all x1, waiting for transfers between devices, local(): lax.all_to_all(keys, 'seq', split_axis=1, concat_axis=0, tiled=True)  19.9 us
    all_to_all x1, waiting for transfers between devices, local(): lax.all_to_all(queries, 'seq', split_axis=1, concat_axis=0, tiled=True)  19.9 us
    sub x3, matrix products, block_step(): exp_scores = jnp.exp(scores - row_max)  18.7 us
    all_to_all x1, waiting for transfers between devices, local(): lax.all_to_all(query_grad_h, 'seq', split_axis=0, concat_axis=1, tiled=True)  16.3 us
    all_to_all x1, waiting for transfers between devices, local(): lax.all_to_all(attn_grad, 'seq', split_axis=1, concat_axis=0, tiled=True)  15.4 us
  transfers between devices with their start and end apart: 19, of which 12 were waited for; matrix products, arithmetic and copies ran while one was open for 28% of the time, Pallas kernels for 0%

profile of v1, /device:TPU:0, one launch (start us, length us, event | category | flops | bytes accessed | tf_op | source)
XLA Modules:
  0.0 419.6 jit_solution(16874646284702356238)
XLA Ops:
  9.2 6.4 %all-to-all-start.1 = ((s32[8,1,192]{2,1,0:T(1,128)}), s32[8,1,192]{2,1,0:T(1,128)S(1)}, u32[]{:S(2)}, u32[]{:S(2)}) async-start(s32[8,1,192]{2,1,0:T(1,128)} %broadcast_in_dim.37), calls=%async_computation.1 | async-start | bytes 16384 | tf_op jit(solution)/shard_map/all_to_all | solution.py:47
  15.6 2.1 copy.118
  17.7 3.5 all-to-all-done.1
  21.2 3.6 all-to-all-start
  25.7 19.9 %all-to-all-done = bf16[192,8,256]{2,0,1:T(8,128)(2,1)S(1)} async-done(((bf16[192,8,256]{2,0,1:T(8,128)(2,1)}), bf16[192,8,256]{2,0,1:T(8,128)(2,1)S(1)}, u32[]{:S(2)}, u32[]{:S(2)}) %all-to-all-start) | async-done | bytes 786464 | tf_op jit(solution)/shard_map/all_to_all | solution.py:40
  45.6 3.5 all-to-all-start.2
  50.1 19.9 %all-to-all-done.2 = bf16[192,8,256]{2,0,1:T(8,128)(2,1)S(1)} async-done(((bf16[192,8,256]{2,0,1:T(8,128)(2,1)}), bf16[192,8,256]{2,0,1:T(8,128)(2,1)S(1)}, u32[]{:S(2)}, u32[]{:S(2)}) %all-to-all-start.2) | async-done | bytes 786464 | tf_op jit(solution)/shard_map/all_to_all | solution.py:41
  70.1 3.5 all-to-all-start.4
  73.6 26.4 %all-gather.3.cloned.1.call-done = bf16[2048,2048]{1,0:T(8,128)(2,1)} async-done(((bf16[512,2048]{1,0:T(8,128)(2,1)}), bf16[2048,2048]{1,0:T(8,128)(2,1)}) %all-gather.3.cloned.1.call-update) | async-done | bytes 8388624 | tf_op jit(solution)/shard_map/all_gather | solution.py:35
  100.1 6.3 %convolution_convert_fusion.1 = bf16[192,2048]{1,0:T(8,128)(2,1)S(1)} fusion(bf16[192,2048]{1,0:T(8,128)(2,1)S(1)} %copy-done.11, bf16[2048,2048]{1,0:T(8,128)(2,1)} %all-gather.3.cloned.1.call-done), kind=kOutput, calls=%fused_computation.32 | convolution fusion | flops 1611005952 | bytes 9961472 | tf_op jit(solution)/shard_map/dot_general | solution.py:33
  107.3 4.6 %all-to-all-start.3 = ((bf16[192,8,256]{2,0,1:T(8,128)(2,1)}), bf16[192,8,256]{2,0,1:T(8,128)(2,1)S(1)}, u32[]{:S(2)}, u32[]{:S(2)}) async-start(bf16[192,8,256]{2,0,1:T(8,128)(2,1)} %bitcast.106), calls=%async_computation.3 | async-start | bytes 1572864 | tf_op jit(solution)/shard_map/all_to_all | solution.py:44
  115.4 2.0 copy.68
  117.5 15.4 %all-to-all-done.3 = bf16[192,8,256]{2,0,1:T(8,128)(2,1)S(1)} async-done(((bf16[192,8,256]{2,0,1:T(8,128)(2,1)}), bf16[192,8,256]{2,0,1:T(8,128)(2,1)S(1)}, u32[]{:S(2)}, u32[]{:S(2)}) %all-to-all-start.3) | async-done | bytes 786464 | tf_op jit(solution)/shard_map/all_to_all | solution.py:44
  133.9 81.1 %while.17 = (s32[]{:T(128)}, f32[1536,2,128]{0,2,1:T(8,128)}, f32[1536,2,128]{0,2,1:T(8,128)}, bf16[3,512,2,128]{3,2,1,0:T(2,128)(2,1)}, bf16[3,512,2,128]{3,2,1...) while((s32[]{:T(128)}, f32[1536,2,128]{0,2,1:T(8,128)}, ...), condition=%wide.region_4.5_spmd.clone, body=%wide.region_0.4_spmd.clone.sunk | while | flops 2435711488 | bytes 117737336 | solution.py:101
  133.9 1.1 constant_dynamic-slice_fusion.6
  135.7 1.1 constant_dynamic-slice_fusion.8
  136.8 6.2 %fusion.55 = (f32[2,512]{1,0:T(2,128)S(1)}, f32[2,512,1536]{2,1,0:T(8,128)}) fusion(pred[512,1536]{1,0:T(8,128)(4,1)S(1)} %compare_or_fusion.2, bf16[1536,2,128]{2,0,1:T(8,128)(2,1)} %get-tuple-element.308, bf16[1,512,2,128]{3,2,1,0:T(2,128)(2,1)S(1)} %constant_dynamic-slice_fusion.8), kind=kOutput, calls=%fused_computation.72.clone.1 | convolution fusion | flops 408946176 | bytes 8130560 | tf_op jit(solution)/shard_map/while/body/eval_jaxpr/sub | solution.py:72
  143.0 3.8 fusion.56
  146.8 3.4 multiply_reduce_fusion.2
  150.2 2.4 multiply_convert_fusion.3
  152.6 2.9 fusion.57
  156.5 2.7 fusion.59
  159.2 1.3 copy_dynamic-update-slice_fusion.3
  160.6 1.1 constant_dynamic-slice_fusion.6
  162.3 1.1 constant_dynamic-slice_fusion.8
  163.5 6.2 %fusion.55 = (f32[2,512]{1,0:T(2,128)S(1)}, f32[2,512,1536]{2,1,0:T(8,128)}) fusion(pred[512,1536]{1,0:T(8,128)(4,1)S(1)} %compare_or_fusion.2, bf16[1536,2,128]{2,0,1:T(8,128)(2,1)} %get-tuple-element.308, bf16[1,512,2,128]{3,2,1,0:T(2,128)(2,1)S(1)} %constant_dynamic-slice_fusion.8), kind=kOutput, calls=%fused_computation.72.clone.1 | convolution fusion | flops 408946176 | bytes 8130560 | tf_op jit(solution)/shard_map/while/body/eval_jaxpr/sub | solution.py:72
  169.7 3.8 fusion.56
  173.5 3.4 multiply_reduce_fusion.2
  176.9 2.4 multiply_convert_fusion.3
  179.3 3.4 fusion.57
  183.7 2.7 fusion.59
  186.4 1.3 copy_dynamic-update-slice_fusion.3
  187.8 1.1 constant_dynamic-slice_fusion.6
  189.5 1.1 constant_dynamic-slice_fusion.8
  190.7 6.2 %fusion.55 = (f32[2,512]{1,0:T(2,128)S(1)}, f32[2,512,1536]{2,1,0:T(8,128)}) fusion(pred[512,1536]{1,0:T(8,128)(4,1)S(1)} %compare_or_fusion.2, bf16[1536,2,128]{2,0,1:T(8,128)(2,1)} %get-tuple-element.308, bf16[1,512,2,128]{3,2,1,0:T(2,128)(2,1)S(1)} %constant_dynamic-slice_fusion.8), kind=kOutput, calls=%fused_computation.72.clone.1 | convolution fusion | flops 408946176 | bytes 8130560 | tf_op jit(solution)/shard_map/while/body/eval_jaxpr/sub | solution.py:72
  196.9 3.8 fusion.56
  200.7 3.4 multiply_reduce_fusion.2
  204.1 2.4 multiply_convert_fusion.3
  206.5 3.4 fusion.57
  210.9 2.7 fusion.59
  213.6 1.3 copy_dynamic-update-slice_fusion.3
  215.0 2.4 reshape_reshape.3
  217.7 1.8 collective-permute-start.2
  219.6 2.4 collective-permute-start.4
  222.1 1.3 collective-permute-start.5
  223.4 2.3 collective-permute-start.6
  225.8 8.7 %collective-permute-done.3 = bf16[192,256]{1,0:T(8,128)(2,1)S(1)} collective-permute-done((bf16[192,256]{1,0:T(8,128)(2,1)S(1)}, bf16[192,256]{1,0:T(8,128)(2,1)S(1)}, u32[]{:S(2)}, u32[]{:S(2)}) %collective-permute-start.3) | collective-permute-done | bytes 98336 | tf_op jit(solution)/shard_map/ppermute | solution.py:26
  238.0 3.7 all-to-all-start.8
  241.7 1.4 all_to_all.121
  243.1 10.5 %all-to-all-done.8 = bf16[192,4,512]{2,0,1:T(8,128)(2,1)S(1)} async-done(((bf16[192,4,512]{2,0,1:T(8,128)(2,1)}), bf16[192,4,512]{2,0,1:T(8,128)(2,1)S(1)}, u32[]{:S(2)}, u32[]{:S(2)}) %all-to-all-start.8) | async-done | bytes 786464 | tf_op jit(solution)/shard_map/all_to_all | solution.py:114
  253.7 5.5 %all-to-all-start.5 = ((bf16[8,192,256]{2,1,0:T(8,128)(2,1)}), bf16[8,192,256]{2,1,0:T(8,128)(2,1)S(1)}, u32[]{:S(2)}, u32[]{:S(2)}) async-start(bf16[8,192,256]{2,1,0:T(8,128)(2,1)} %all_to_all.121), calls=%async_computation.5 | async-start | bytes 1572864 | tf_op jit(solution)/shard_map/all_to_all | solution.py:110
  260.2 2.2 copy.71
  262.4 1.4 all_to_all.125
  263.8 16.3 %all-to-all-done.5 = bf16[8,192,256]{2,1,0:T(8,128)(2,1)S(1)} async-done(((bf16[8,192,256]{2,1,0:T(8,128)(2,1)}), bf16[8,192,256]{2,1,0:T(8,128)(2,1)S(1)}, u32[]{:S(2)}, u32[]{:S(2)}) %all-to-all-start.5) | async-done | bytes 786464 | tf_op jit(solution)/shard_map/all_to_all | solution.py:110
  280.1 4.2 %all-to-all-start.6 = ((bf16[8,192,256]{2,1,0:T(8,128)(2,1)}), bf16[8,192,256]{2,1,0:T(8,128)(2,1)}, u32[]{:S(2)}, u32[]{:S(2)}) async-start(bf16[8,192,256]{2,1,0:T(8,128)(2,1)} %all_to_all.125), calls=%async_computation.6 | async-start | bytes 1572864 | tf_op jit(solution)/shard_map/all_to_all | solution.py:111
  284.4 5.7 %fusion.21 = f32[512,2048]{1,0:T(8,128)} fusion(bf16[768,512]{1,0:T(8,128)(2,1)S(1)} %bitcast.150, bf16[768,2048]{1,0:T(8,128)(2,1)} %all-gather.5.cloned.1.call-done), kind=kOutput, calls=%fused_computation.73 | convolution fusion | flops 1610612736 | bytes 8126464 | tf_op jit(solution)/shard_map/dot_general | solution.py:116
  290.2 1.4 copy-done.6
  292.2 1.4 all_to_all.129
  293.6 15.4 %all-to-all-done.6 = bf16[8,192,256]{2,1,0:T(8,128)(2,1)} async-done(((bf16[8,192,256]{2,1,0:T(8,128)(2,1)}), bf16[8,192,256]{2,1,0:T(8,128)(2,1)}, u32[]{:S(2)}, u32[]{:S(2)}) %all-to-all-start.6) | async-done | bytes 786464 | tf_op jit(solution)/shard_map/all_to_all | solution.py:111
  309.0 3.5 all-to-all-start.7
  313.5 2.1 copy.93
  315.7 26.6 %all-to-all-done.7 = bf16[8,192,256]{2,1,0:T(8,128)(2,1)S(1)} async-done(((bf16[8,192,256]{2,1,0:T(8,128)(2,1)}), bf16[8,192,256]{2,1,0:T(8,128)(2,1)S(1)}, u32[]{:S(2)}, u32[]{:S(2)}) %all-to-all-start.7) | async-done | bytes 786464 | tf_op jit(solution)/shard_map/all_to_all | solution.py:112
  343.3 65.1 %all-reduce.2.cloned.1.call-done = f32[512,2048]{1,0:T(8,128)} async-done(((f32[512,2048]{1,0:T(8,128)}), f32[512,2048]{1,0:T(8,128)}) %all-reduce.2.cloned.1.call-update) | async-done | bytes 4194320 | tf_op jit(solution)/shard_map/psum | solution.py:115
  408.4 4.7 %copy.156 = f32[512,2048]{1,0:T(8,128)} copy(f32[512,2048]{1,0:T(8,128)} %all-reduce.2.cloned.1.call-done) | data formatting | bytes 8388608
  (118 shorter events, 21.7 us)
Async XLA Ops:
  7.2 17.6 %copy-start.9 = (bf16[192,2048]{1,0:T(8,128)(2,1)S(1)}, bf16[192,2048]{1,0:T(8,128)(2,1)}, u32[]{:S(2)}) copy-start(bf16[192,2048]{1,0:T(8,128)(2,1)} %param.10) | copy-start | bytes 2359300
  7.2 92.9 %all-gather.3.cloned.1.call-start = ((), (), s32[]{:S(2)}) async-start(), calls=%async_computation.9 | async-start | bytes 10485760 | tf_op jit(solution)/shard_map/all_gather | solution.py:35
  9.2 12.0 %all-to-all-start.1 = ((s32[8,1,192]{2,1,0:T(1,128)}), s32[8,1,192]{2,1,0:T(1,128)S(1)}, u32[]{:S(2)}, u32[]{:S(2)}) async-start(s32[8,1,192]{2,1,0:T(1,128)} %broadcast_in_dim.37), calls=%async_computation.1 | async-start | bytes 16384 | tf_op jit(solution)/shard_map/all_to_all | solution.py:47
  15.6 33.6 %copy-start.10 = (bf16[192,2048]{1,0:T(8,128)(2,1)S(1)}, bf16[192,2048]{1,0:T(8,128)(2,1)}, u32[]{:S(2)}) copy-start(bf16[192,2048]{1,0:T(8,128)(2,1)} %param.11) | copy-start | bytes 2359300
  21.2 24.5 %all-to-all-start = ((bf16[192,8,256]{2,0,1:T(8,128)(2,1)}), bf16[192,8,256]{2,0,1:T(8,128)(2,1)S(1)}, u32[]{:S(2)}, u32[]{:S(2)}) async-start(bf16[192,8,256]{2,0,1:T(8,128)(2,1)} %bitcast.108), calls=%async_computation | async-start | bytes 1572864 | tf_op jit(solution)/shard_map/all_to_all | solution.py:40
  24.8 75.3 %copy-start.11 = (bf16[192,2048]{1,0:T(8,128)(2,1)S(1)}, bf16[192,2048]{1,0:T(8,128)(2,1)}, u32[]{:S(2)}) copy-start(bf16[192,2048]{1,0:T(8,128)(2,1)} %param.12) | copy-start | bytes 2359300
  45.6 24.4 %all-to-all-start.2 = ((bf16[192,8,256]{2,0,1:T(8,128)(2,1)}), bf16[192,8,256]{2,0,1:T(8,128)(2,1)S(1)}, u32[]{:S(2)}, u32[]{:S(2)}) async-start(bf16[192,8,256]{2,0,1:T(8,128)(2,1)} %bitcast.107), calls=%async_computation.2 | async-start | bytes 1572864 | tf_op jit(solution)/shard_map/all_to_all | solution.py:41
  70.1 37.2 %all-to-all-start.4 = ((bf16[192,8,256]{2,0,1:T(8,128)(2,1)}), bf16[192,8,256]{2,0,1:T(8,128)(2,1)S(1)}, u32[]{:S(2)}, u32[]{:S(2)}) async-start(bf16[192,8,256]{2,0,1:T(8,128)(2,1)} %bitcast.105), calls=%async_computation.4 | async-start | bytes 1572864 | tf_op jit(solution)/shard_map/all_to_all | solution.py:42
  107.3 25.6 %all-to-all-start.3 = ((bf16[192,8,256]{2,0,1:T(8,128)(2,1)}), bf16[192,8,256]{2,0,1:T(8,128)(2,1)S(1)}, u32[]{:S(2)}, u32[]{:S(2)}) async-start(bf16[192,8,256]{2,0,1:T(8,128)(2,1)} %bitcast.106), calls=%async_computation.3 | async-start | bytes 1572864 | tf_op jit(solution)/shard_map/all_to_all | solution.py:44
  111.9 172.5 %all-gather.5.cloned.1.call-start = ((), (), s32[]{:S(2)}) async-start(), calls=%async_computation.10 | async-start | bytes 3932160 | tf_op jit(solution)/shard_map/all_gather | solution.py:52
  136.8 6.2 %copy-start.7 = (bf16[1,512,2,128]{3,2,1,0:T(2,128)(2,1)}, bf16[1,512,2,128]{3,2,1,0:T(2,128)(2,1)S(1)}, u32[]{:S(2)}) copy-start(bf16[1,512,2,128]{3,2,1,0:T(2,128)(2,1)S(1)} %constant_dynamic-slice_fusion.8) | copy-start | bytes 786436 | tf_op jit(solution)/shard_map/while
  143.0 7.2 %copy-start.2 = (f32[2,512,1536]{2,1,0:T(8,128)S(1)}, f32[2,512,1536]{2,1,0:T(8,128)}, u32[]{:S(2)}) copy-start(f32[2,512,1536]{2,1,0:T(8,128)} %get-tuple-element.265) | copy-start | bytes 18874372 | tf_op jit(solution)/shard_map/while
  146.8 5.8 %copy-start = (bf16[2,512,1536]{2,1,0:T(8,128)(2,1)}, bf16[2,512,1536]{2,1,0:T(8,128)(2,1)S(1)}, u32[]{:S(2)}) copy-start(bf16[2,512,1536]{2,1,0:T(8,128)(2,1)S(1)} %fusion.56) | copy-start | bytes 9437188 | tf_op jit(solution)/shard_map/while
  152.6 2.9 copy-start.1
  152.6 2.9 copy-start.4
  156.5 4.1 copy-start.5
  156.5 2.7 copy-start.8
  163.5 6.2 %copy-start.7 = (bf16[1,512,2,128]{3,2,1,0:T(2,128)(2,1)}, bf16[1,512,2,128]{3,2,1,0:T(2,128)(2,1)S(1)}, u32[]{:S(2)}) copy-start(bf16[1,512,2,128]{3,2,1,0:T(2,128)(2,1)S(1)} %constant_dynamic-slice_fusion.8) | copy-start | bytes 786436 | tf_op jit(solution)/shard_map/while
  169.7 7.2 %copy-start.2 = (f32[2,512,1536]{2,1,0:T(8,128)S(1)}, f32[2,512,1536]{2,1,0:T(8,128)}, u32[]{:S(2)}) copy-start(f32[2,512,1536]{2,1,0:T(8,128)} %get-tuple-element.265) | copy-start | bytes 18874372 | tf_op jit(solution)/shard_map/while
  173.4 5.8 %copy-start = (bf16[2,512,1536]{2,1,0:T(8,128)(2,1)}, bf16[2,512,1536]{2,1,0:T(8,128)(2,1)S(1)}, u32[]{:S(2)}) copy-start(bf16[2,512,1536]{2,1,0:T(8,128)(2,1)S(1)} %fusion.56) | copy-start | bytes 9437188 | tf_op jit(solution)/shard_map/while
  179.3 3.5 copy-start.1
  179.3 3.4 copy-start.4
  183.7 4.1 copy-start.5
  183.7 2.7 copy-start.8
  190.7 6.2 %copy-start.7 = (bf16[1,512,2,128]{3,2,1,0:T(2,128)(2,1)}, bf16[1,512,2,128]{3,2,1,0:T(2,128)(2,1)S(1)}, u32[]{:S(2)}) copy-start(bf16[1,512,2,128]{3,2,1,0:T(2,128)(2,1)S(1)} %constant_dynamic-slice_fusion.8) | copy-start | bytes 786436 | tf_op jit(solution)/shard_map/while
  196.9 7.2 %copy-start.2 = (f32[2,512,1536]{2,1,0:T(8,128)S(1)}, f32[2,512,1536]{2,1,0:T(8,128)}, u32[]{:S(2)}) copy-start(f32[2,512,1536]{2,1,0:T(8,128)} %get-tuple-element.265) | copy-start | bytes 18874372 | tf_op jit(solution)/shard_map/while
  200.7 5.8 %copy-start = (bf16[2,512,1536]{2,1,0:T(8,128)(2,1)}, bf16[2,512,1536]{2,1,0:T(8,128)(2,1)S(1)}, u32[]{:S(2)}) copy-start(bf16[2,512,1536]{2,1,0:T(8,128)(2,1)S(1)} %fusion.56) | copy-start | bytes 9437188 | tf_op jit(solution)/shard_map/while
  206.5 3.5 copy-start.1
  206.5 3.4 copy-start.4
  210.9 4.1 copy-start.5
  210.9 2.7 copy-start.8
  217.5 4.6 %collective-permute-start = (bf16[192,256]{1,0:T(8,128)(2,1)S(1)}, bf16[192,256]{1,0:T(8,128)(2,1)S(1)}, u32[]{:S(2)}, u32[]{:S(2)}) collective-permute-start(bf16[192,256]{1,0:T(8,128)(2,1)S(1)} %get-tuple-element.184), channel_id=1, source_target_pairs={{0,1},{1,0},{2,3},{3,2},{4,5},{5,4},{6,7},{7,6},{8,9},{9,8},{10,11... | collective-permute-start | bytes 294920 | tf_op jit(solution)/shard_map/ppermute | solution.py:26
  217.6 5.8 %collective-permute-start.1 = (bf16[192,256]{1,0:T(8,128)(2,1)S(1)}, bf16[192,256]{1,0:T(8,128)(2,1)S(1)}, u32[]{:S(2)}, u32[]{:S(2)}) collective-permute-start(bf16[192,256]{1,0:T(8,128)(2,1)S(1)} %get-tuple-element.183), channel_id=1, source_target_pairs={{0,2},{1,3},{2,0},{3,1},{4,6},{5,7},{6,4},{7,5},{8,10},{9,11},{10,... | collective-permute-start | bytes 294920 | tf_op jit(solution)/shard_map/ppermute | solution.py:26
  217.7 8.0 %collective-permute-start.2 = (bf16[192,256]{1,0:T(8,128)(2,1)S(1)}, bf16[192,256]{1,0:T(8,128)(2,1)S(1)}, u32[]{:S(2)}, u32[]{:S(2)}) collective-permute-start(bf16[192,256]{1,0:T(8,128)(2,1)S(1)} %get-tuple-element.182), channel_id=1, source_target_pairs={{0,3},{1,2},{2,1},{3,0},{4,7},{5,6},{6,5},{7,4},{8,11},{9,10},{10,... | collective-permute-start | bytes 294920 | tf_op jit(solution)/shard_map/ppermute | solution.py:26
  219.4 15.0 %collective-permute-start.3 = (bf16[192,256]{1,0:T(8,128)(2,1)S(1)}, bf16[192,256]{1,0:T(8,128)(2,1)S(1)}, u32[]{:S(2)}, u32[]{:S(2)}) collective-permute-start(bf16[192,256]{1,0:T(8,128)(2,1)S(1)} %get-tuple-element.181), channel_id=1, source_target_pairs={{0,4},{1,5},{2,6},{3,7},{4,0},{5,1},{6,2},{7,3},{8,12},{9,13},{10,... | collective-permute-start | bytes 294920 | tf_op jit(solution)/shard_map/ppermute | solution.py:26
  219.6 15.7 %collective-permute-start.4 = (bf16[192,256]{1,0:T(8,128)(2,1)S(1)}, bf16[192,256]{1,0:T(8,128)(2,1)S(1)}, u32[]{:S(2)}, u32[]{:S(2)}) collective-permute-start(bf16[192,256]{1,0:T(8,128)(2,1)S(1)} %get-tuple-element.180), channel_id=1, source_target_pairs={{0,5},{1,4},{2,7},{3,6},{4,1},{5,0},{6,3},{7,2},{8,13},{9,12},{10,... | collective-permute-start | bytes 294920 | tf_op jit(solution)/shard_map/ppermute | solution.py:26
  222.1 13.3 %collective-permute-start.5 = (bf16[192,256]{1,0:T(8,128)(2,1)S(1)}, bf16[192,256]{1,0:T(8,128)(2,1)S(1)}, u32[]{:S(2)}, u32[]{:S(2)}) collective-permute-start(bf16[192,256]{1,0:T(8,128)(2,1)S(1)} %get-tuple-element.179), channel_id=1, source_target_pairs={{0,6},{1,7},{2,4},{3,5},{4,2},{5,3},{6,0},{7,1},{8,14},{9,15},{10,... | collective-permute-start | bytes 294920 | tf_op jit(solution)/shard_map/ppermute | solution.py:26
  223.4 12.0 %collective-permute-start.6 = (bf16[192,256]{1,0:T(8,128)(2,1)S(1)}, bf16[192,256]{1,0:T(8,128)(2,1)S(1)}, u32[]{:S(2)}, u32[]{:S(2)}) collective-permute-start(bf16[192,256]{1,0:T(8,128)(2,1)S(1)} %get-tuple-element.178), channel_id=1, source_target_pairs={{0,7},{1,6},{2,5},{3,4},{4,3},{5,2},{6,1},{7,0},{8,15},{9,14},{10,... | collective-permute-start | bytes 294920 | tf_op jit(solution)/shard_map/ppermute | solution.py:26
  236.0 5.7 %copy-start.12 = (bf16[3,512,2,128]{3,2,1,0:T(2,128)(2,1)S(1)}, bf16[3,512,2,128]{3,2,1,0:T(2,128)(2,1)}, u32[]{:S(2)}) copy-start(bf16[3,512,2,128]{3,2,1,0:T(2,128)(2,1)} %get-tuple-element.69) | copy-start | bytes 2359300
  237.0 22.2 %copy-start.3 = (f32[1536,2,128]{0,2,1:T(8,128)S(1)}, f32[1536,2,128]{0,2,1:T(8,128)}, u32[]{:S(2)}) copy-start(f32[1536,2,128]{0,2,1:T(8,128)} %get-tuple-element.70) | copy-start | bytes 4718596
  238.0 15.7 %all-to-all-start.8 = ((bf16[192,4,512]{2,0,1:T(8,128)(2,1)}), bf16[192,4,512]{2,0,1:T(8,128)(2,1)S(1)}, u32[]{:S(2)}, u32[]{:S(2)}) async-start(bf16[192,4,512]{2,0,1:T(8,128)(2,1)} %copy.77), calls=%async_computation.8 | async-start | bytes 1572864 | tf_op jit(solution)/shard_map/all_to_all | solution.py:114
  253.7 26.5 %all-to-all-start.5 = ((bf16[8,192,256]{2,1,0:T(8,128)(2,1)}), bf16[8,192,256]{2,1,0:T(8,128)(2,1)S(1)}, u32[]{:S(2)}, u32[]{:S(2)}) async-start(bf16[8,192,256]{2,1,0:T(8,128)(2,1)} %all_to_all.121), calls=%async_computation.5 | async-start | bytes 1572864 | tf_op jit(solution)/shard_map/all_to_all | solution.py:110
  280.1 28.9 %all-to-all-start.6 = ((bf16[8,192,256]{2,1,0:T(8,128)(2,1)}), bf16[8,192,256]{2,1,0:T(8,128)(2,1)}, u32[]{:S(2)}, u32[]{:S(2)}) async-start(bf16[8,192,256]{2,1,0:T(8,128)(2,1)} %all_to_all.125), calls=%async_computation.6 | async-start | bytes 1572864 | tf_op jit(solution)/shard_map/all_to_all | solution.py:111
  284.3 124.1 %all-reduce.2.cloned.1.call-start = ((), (), s32[]{:S(2)}) async-start(), calls=%async_computation.11 | async-start | bytes 8388608 | tf_op jit(solution)/shard_map/psum | solution.py:115
  290.1 1.4 copy-start.6
  309.0 33.3 %all-to-all-start.7 = ((bf16[8,192,256]{2,1,0:T(8,128)(2,1)}), bf16[8,192,256]{2,1,0:T(8,128)(2,1)S(1)}, u32[]{:S(2)}, u32[]{:S(2)}) async-start(bf16[8,192,256]{2,1,0:T(8,128)(2,1)} %all_to_all.129), calls=%async_computation.7 | async-start | bytes 1572864 | tf_op jit(solution)/shard_map/all_to_all | solution.py:112
Sparse Core Ops, SparseCore 0:
  9.8 90.1 all-gather.2
  114.6 44.3 all-gather.4
  290.3 118.0 all-reduce.1
